TPU v7x, 256 devices: a whole 4x4x8 slice. The times are simulated.
256 devices in a mesh: attn: 32 (over z, y), expert: 4 (over x), rep: 2 (over core).
Axes of the slice: x: 4, y: 4, z: 8, core: 2. Of those that a mesh axis runs over, the one named last changes fastest.
Arguments:
- queries: bfloat16 [256, 73728], P('attn', ('expert', 'rep')), may hold values from -120 to 120
- new_latent: bfloat16 [256, 576], P('attn'), may hold values from -6 to 6
- cache_pool: bfloat16 [16384, 576], P('attn'), may hold values from -6 to 6
- local_len: int32 [32, 4], P('attn'), may hold values from 1 to 384, 512 in all within a row
- spill_cache: bfloat16 [1024, 16, 576], P('attn'), may hold values from -6 to 6
- spill_owner: int32 [1024], replicated, may hold values from -1 to 127, as said below
- w_uv: bfloat16 [128, 512, 128], P(('expert', 'rep')), may hold values from -0.25 to 0.25
- w_o: bfloat16 [16384, 7168], P(('expert', 'rep'), 'attn'), may hold values from -0.046875 to 0.046875
- residual: bfloat16 [256, 7168], P(None, 'attn'), may hold values from -3 to 3
- norm_gain: float32 [7168], replicated, may hold values from 0.5 to 1.5
- route_ids: int32 [256, 4], replicated, may hold values from 0 to 15, all different within a row; in each aligned block of 128 rows (0 to 127, 128 to 255, ...) at most 40 rows name the same one
- route_scores: float32 [256, 4], replicated, may hold values from 0.05 to 1
- w_gate: bfloat16 [7168, 32768], P(None, ('attn', 'expert')), may hold values from -0.0625 to 0.0625
- w_up: bfloat16 [7168, 32768], P(None, ('attn', 'expert')), may hold values from -0.0625 to 0.0625
- w_down: bfloat16 [32768, 7168], P(('attn', 'expert')), may hold values from -0.125 to 0.125
Outputs:
- mixed: bfloat16 [256, 7168], P('rep', ('attn', 'expert'))
Inputs may be any that keep to these rules, and one draw needn't show every extreme that they name: Each row of local_len sums to 512. `spill_owner`: each entry is -1 or the number of a request that lives on another index of attn than the block's slot. The slots of one index of attn hold at most 2 blocks of the requests of any one other index, and some index holds exactly 2 for some other index in every draw. `route_ids`: the token rows fall into 2 aligned blocks of 128 rows in order (2 being the size of rep); in each block no expert is named by more than 40 rows, and in some block one is named by exactly 40.
All inputs are finite; a program needn't handle non-finite values.
Results may differ from a plain program's by a relative error of at most 0.025.
Values may be sent and summed in bfloat16 or wider, within the bound.
No kernel may reach another device: no remote copies, remote signals or barrier semaphores. Data moves between devices by JAX's collectives and lax.ppermute only.
A program may use at most 128 MiB of HBM per device.

v0:
```python
import jax
import jax.numpy as jnp
from jax import lax
from jax.sharding import PartitionSpec as P

ROPE = 64
VH = 128
EXPERTS = 16
TOP = 4
MAXLOC = 384
CAP = 2
floor_score = -1e30
scale_out = 2.5


def expert_tables(route_ids, part_index, part_count, capacity):
    row_count = route_ids.shape[0] // part_count
    route_part = lax.dynamic_slice_in_dim(route_ids, part_index * row_count, row_count, 0)
    member = jnp.any(
        route_part[:, :, None] == jnp.arange(EXPERTS, dtype=jnp.int32)[None, None, :], axis=1
    )
    order_rank = jnp.cumsum(member.astype(jnp.int32), axis=0) - 1
    slot_ids = jnp.arange(capacity, dtype=jnp.int32)
    slot_hit = member[None, :, :] & (order_rank[None, :, :] == slot_ids[:, None, None])
    place_ids = jnp.arange(row_count, dtype=jnp.int32)
    slot_token = jnp.sum(jnp.where(slot_hit, place_ids[None, :, None], 0), axis=1)
    filled = jnp.any(slot_hit, axis=1)
    return (slot_token.T, filled.T, route_part)


def per_device(
    queries,
    new_latent,
    cache_pool,
    local_len,
    spill_cache,
    spill_owner,
    w_uv,
    w_o,
    residual,
    norm_gain,
    route_ids,
    route_scores,
    w_gate,
    w_up,
    w_down,
):
    n_attn = lax.axis_size("attn")
    n_expert = lax.axis_size("expert")
    n_rep = lax.axis_size("rep")
    attn_here = lax.axis_index("attn")
    expert_here = lax.axis_index("expert")
    rep_here = lax.axis_index("rep")
    req_count = local_len.shape[1]
    head_count = w_uv.shape[0]
    row_width = new_latent.shape[1]
    lat_width = w_uv.shape[1]
    score_scale = float(VH + ROPE) ** (-0.5)
    query_rows = queries.reshape(req_count, 2, head_count, row_width)
    lengths = local_len[0]
    starts = jnp.cumsum(lengths) - lengths
    padded = jnp.concatenate([cache_pool, jnp.zeros((MAXLOC, row_width), cache_pool.dtype)], axis=0)
    windows = jax.vmap(lambda start_one: lax.dynamic_slice_in_dim(padded, start_one, MAXLOC, 0))(
        starts
    )
    local_scores = (
        jnp.einsum("rthc,rkc->rthk", query_rows, windows, preferred_element_type=jnp.float32)
        * score_scale
    )
    inside = jnp.arange(MAXLOC)[None, :] < lengths[:, None]
    local_scores = jnp.where(inside[:, None, None, :], local_scores, floor_score)
    fresh_keys = new_latent.reshape(req_count, 2, row_width)
    fresh_scores = (
        jnp.einsum("rthc,rkc->rthk", query_rows, fresh_keys, preferred_element_type=jnp.float32)
        * score_scale
    )
    causal = jnp.arange(2)[None, :] <= jnp.arange(2)[:, None]
    fresh_scores = jnp.where(causal[None, :, None, :], fresh_scores, floor_score)
    spill_count = spill_cache.shape[0]
    directory = spill_owner.reshape(n_attn, spill_count)
    owner_dev = jnp.where(directory >= 0, directory // req_count, -1)
    earlier = jnp.arange(spill_count)[:, None] > jnp.arange(spill_count)[None, :]
    same_owner = owner_dev[:, :, None] == owner_dev[:, None, :]
    order_rank = jnp.sum(same_owner & earlier[None, :, :], axis=2)
    slot_ids = jnp.arange(CAP)
    own_row = owner_dev[attn_here]
    own_rank = order_rank[attn_here]
    pick_slot = (own_row[None, None, :] == jnp.arange(n_attn)[:, None, None]) & (
        own_rank[None, None, :] == slot_ids[None, :, None]
    )
    outgoing = jnp.einsum(
        "dks,sbc->dkbc",
        pick_slot.astype(jnp.bfloat16),
        spill_cache,
        preferred_element_type=jnp.float32,
    ).astype(jnp.bfloat16)
    incoming = lax.all_to_all(outgoing, "attn", split_axis=0, concat_axis=0, tiled=True)
    mine_slot = (owner_dev[:, None, :] == attn_here) & (
        order_rank[:, None, :] == slot_ids[None, :, None]
    )
    present = jnp.any(mine_slot, axis=2).reshape(-1)
    request = jnp.sum(
        jnp.where(mine_slot, directory[:, None, :] - attn_here * req_count, 0), axis=2
    ).reshape(-1)
    blocks = incoming.reshape(n_attn * CAP, incoming.shape[2], row_width)
    slot_query = jnp.take(query_rows, request, axis=0)
    spill_scores = (
        jnp.einsum("nthc,nbc->nthb", slot_query, blocks, preferred_element_type=jnp.float32)
        * score_scale
    )
    spill_scores = jnp.where(present[:, None, None, None], spill_scores, floor_score)
    belong = (request[None, :] == jnp.arange(req_count)[:, None]) & present[None, :]
    spill_top = jnp.max(
        jnp.where(belong[:, :, None, None], jnp.max(spill_scores, axis=3)[None], floor_score),
        axis=1,
    )
    row_top = jnp.maximum(
        jnp.maximum(jnp.max(local_scores, axis=3), jnp.max(fresh_scores, axis=3)), spill_top
    )
    local_weight = jnp.exp(local_scores - row_top[..., None])
    fresh_weight = jnp.exp(fresh_scores - row_top[..., None])
    spill_weight = jnp.exp(spill_scores - jnp.take(row_top, request, axis=0)[..., None])
    spill_weight = jnp.where(present[:, None, None, None], spill_weight, 0.0)
    belong_f = belong.astype(jnp.float32)
    denominator = jnp.sum(local_weight, axis=3) + jnp.sum(fresh_weight, axis=3)
    denominator = denominator + jnp.einsum(
        "rn,nth->rth", belong_f, jnp.sum(spill_weight, axis=3), precision=lax.Precision.HIGHEST
    )
    numerator = jnp.einsum(
        "rthk,rkc->rthc",
        local_weight.astype(jnp.bfloat16),
        windows[:, :, :lat_width],
        preferred_element_type=jnp.float32,
    )
    numerator = numerator + jnp.einsum(
        "rthk,rkc->rthc",
        fresh_weight.astype(jnp.bfloat16),
        fresh_keys[:, :, :lat_width],
        preferred_element_type=jnp.float32,
    )
    spill_numer = jnp.einsum(
        "nthb,nbc->nthc",
        spill_weight.astype(jnp.bfloat16),
        blocks[:, :, :lat_width],
        preferred_element_type=jnp.float32,
    )
    numerator = numerator + jnp.einsum(
        "rn,nthc->rthc", belong_f, spill_numer, precision=lax.Precision.HIGHEST
    )
    attended = (numerator / denominator[..., None]).astype(jnp.bfloat16)
    values = jnp.einsum(
        "rthc,hcv->rthv", attended, w_uv, preferred_element_type=jnp.float32
    ).astype(jnp.bfloat16)
    values = values.reshape(2 * req_count, head_count * w_uv.shape[2])
    partial_cols = jnp.dot(
        lax.all_gather(values, "attn", axis=0, tiled=True), w_o, preferred_element_type=jnp.float32
    )
    attn_cols = lax.psum(partial_cols.astype(jnp.bfloat16), ("expert", "rep")).astype(jnp.float32)
    hidden_cols = (residual.astype(jnp.float32) + attn_cols).astype(jnp.bfloat16)
    rows_part = route_ids.shape[0] // n_rep
    capacity = rows_part * TOP // EXPERTS * 5 // 4
    shards = n_attn * n_expert // EXPERTS
    slot_token, filled, route_part = expert_tables(route_ids, rep_here, n_rep, capacity)
    part_cols = lax.dynamic_slice_in_dim(hidden_cols, rep_here * rows_part, rows_part, 0)
    dest_expert = (jnp.arange(n_attn) * n_expert + expert_here) // shards
    send_rows = jnp.take(slot_token, dest_expert, axis=0)
    send_ok = jnp.take(filled, dest_expert, axis=0)
    outgoing_rows = jnp.where(
        send_ok[:, :, None], jnp.take(part_cols, send_rows, axis=0), jnp.zeros((), jnp.bfloat16)
    )
    outgoing_rows = outgoing_rows[:, :, None, :]
    received = lax.all_to_all(outgoing_rows, "attn", split_axis=0, concat_axis=2, tiled=True)
    item_count = received.shape[1]
    full_rows = received.reshape(item_count, -1)
    widened = full_rows.astype(jnp.float32)
    normed = (
        widened * lax.rsqrt(jnp.mean(widened * widened, axis=1, keepdims=True) + 1e-06) * norm_gain
    ).astype(jnp.bfloat16)
    gate_proj = jnp.dot(normed, w_gate, preferred_element_type=jnp.float32)
    up_proj = jnp.dot(normed, w_up, preferred_element_type=jnp.float32)
    activated = (jax.nn.silu(gate_proj) * up_proj).astype(jnp.bfloat16)
    result = jnp.dot(activated, w_down, preferred_element_type=jnp.float32)
    returned_block = lax.all_to_all(
        result.reshape(1, item_count, n_attn * n_expert, -1).astype(jnp.bfloat16),
        ("attn", "expert"),
        split_axis=2,
        concat_axis=0,
        tiled=True,
    ).astype(jnp.float32)
    returned = returned_block.reshape(n_attn * n_expert, item_count, -1)
    share_part = lax.dynamic_slice_in_dim(route_scores, rep_here * rows_part, rows_part, 0)
    share_part = share_part / jnp.sum(share_part, axis=1, keepdims=True)
    share_table = jnp.sum(
        jnp.where(
            route_part[:, :, None] == jnp.arange(EXPERTS, dtype=jnp.int32)[None, None, :],
            share_part[:, :, None],
            0.0,
        ),
        axis=1,
    )
    source_expert = jnp.arange(n_attn * n_expert) // shards
    back_rows = jnp.take(slot_token, source_expert, axis=0)
    back_ok = jnp.take(filled, source_expert, axis=0)
    weight_coef = (
        jnp.where(back_ok, share_table[back_rows, source_expert[:, None]], 0.0) * scale_out
    )
    sub_cols = returned.shape[2]
    weighted = (weight_coef[:, :, None] * returned).reshape(-1, sub_cols)
    routed = jax.ops.segment_sum(weighted, back_rows.reshape(-1), num_segments=rows_part)
    own_cols = lax.dynamic_slice_in_dim(part_cols, expert_here * sub_cols, sub_cols, 1)
    return (own_cols.astype(jnp.float32) + routed).astype(jnp.bfloat16)


def solution(mesh):
    return jax.shard_map(
        per_device,
        mesh=mesh,
        in_specs=(
            P("attn", ("expert", "rep")),
            P("attn", None),
            P("attn", None),
            P("attn", None),
            P("attn", None, None),
            P(),
            P(("expert", "rep"), None, None),
            P(("expert", "rep"), "attn"),
            P(None, "attn"),
            P(),
            P(),
            P(),
            P(None, ("attn", "expert")),
            P(None, ("attn", "expert")),
            P(("attn", "expert"), None),
        ),
        out_specs=P("rep", ("attn", "expert")),
        check_vma=False,
    )
```

profile of v0, /device:TPU:1, one launch (start us, length us, event | category | flops | bytes accessed | tf_op | source)
XLA Modules:
  0.0 364.1 jit_solution(18145144369421537697)
XLA Ops:
  6.5 0.9 reshape.649
  7.5 0.8 convert_reduce_fusion
  8.3 1.6 convolution_convert_fusion.1
  9.9 1.5 copy.175
  11.4 12.3 %all-to-all-start = ((bf16[32,2,16,576]{3,2,1,0:T(8,128)(2,1)}), bf16[32,2,16,576]{3,2,1,0:T(8,128)(2,1)}, u32[]{:S(2)}, u32[]{:S(2)}) async-start(bf16[32,2,16,576]{3,2,1,0:T(8,128)(2,1)} %copy.175), calls=%async_computation | async-start | bytes 2621440 | tf_op jit(solution)/shard_map/all_to_all | solution.py:97
  25.2 1.1 copy.169
  26.3 2.4 gather_fusion
  28.6 1.2 concatenate.9
  30.3 8.1 %while.1 = (s32[]{:T(128)}, bf16[896,576]{1,0:T(8,128)(2,1)S(1)}, s32[4,2]{0,1:T(2,128)S(1)}, bf16[4,384,576]{2,1,0:T(8,128)(2,1)}, s32[]{:T(128)}) while((s32[]{:T(128)}, bf16[896,576]{1,0:T(8,128)(2,1)S(1)}, s32[4,2]{0,1:T(2,128)S(1)}, bf16[4,384,576]{2,1,0:T(8,128)(2,1)}, s32[]{:T(128)}) %tuple.22), condition=%wide.while_cond, body=%wide.while_body.sunk | while | flops 2 | bytes 935001 | solution.py:63
  30.9 1.5 bitcast_dynamic-update-slice_fusion.2
  32.9 1.5 bitcast_dynamic-update-slice_fusion.2
  34.9 1.4 bitcast_dynamic-update-slice_fusion.2
  36.9 1.5 bitcast_dynamic-update-slice_fusion.2
  38.4 3.0 fusion.93
  41.3 14.2 %all-to-all-done = bf16[32,2,16,576]{3,2,1,0:T(8,128)(2,1)} async-done(((bf16[32,2,16,576]{3,2,1,0:T(8,128)(2,1)}), bf16[32,2,16,576]{3,2,1,0:T(8,128)(2,1)}, u32[]{:S(2)}, u32[]{:S(2)}) %all-to-all-start) | async-done | bytes 1179680 | tf_op jit(solution)/shard_map/all_to_all | solution.py:97
  55.6 6.0 %fusion.2 = f32[64,2,16,16]{2,3,1,0:T(8,128)S(1)} fusion(bf16[64,16,576,1]{2,1,3,0:T(8,128)(2,1)} %bitcast.13, bf16[64,2,16,576]{3,2,1,0:T(8,128)(2,1)} %gather_fusion, pred[64]{0:T(512)(128)(4,1)S(1)} %compare_and_fusion.3), kind=kOutput, calls=%fused_computation.14 | convolution fusion | flops 38928384 | bytes 3670080 | tf_op jit(solution)/shard_map/nthc,nbc->nthb/dot_general | solution.py:108
  63.1 1.1 fusion.51
  64.7 0.9 copy.180
  65.5 1.9 fusion.43
  67.5 3.8 %fusion = f32[4,2,16,512]{3,0,2,1:T(4,128)S(1)} fusion(f32[64,2,16,512]{3,2,1,0:T(8,128)S(1)} %fusion.43, pred[4,64]{1,0:T(4,128)(4,1)S(1)} %fusion.81), kind=kOutput, calls=%fused_computation.12 | convolution fusion | flops 50331648 | bytes 4456704 | tf_op jit(solution)/shard_map/rn,nthc->rthc/dot_general | solution.py:147
  73.7 0.8 select_reduce_fusion
  75.4 0.8 fusion.47
  76.9 67.3 %all-gather.2.cloned.1.call-done = bf16[256,2048]{1,0:T(8,128)(2,1)} async-done(((bf16[8,2048]{1,0:T(8,128)(2,1)}), bf16[256,2048]{1,0:T(8,128)(2,1)}) %all-gather.2.cloned.1.call-update) | async-done | bytes 1048592 | tf_op jit(solution)/shard_map/all_gather | solution.py:156
  144.2 2.4 convolution_convert_fusion.2
  146.6 64.4 %all-reduce.4.cloned.1.call-done = bf16[256,224]{0,1:T(8,128)(2,1)} async-done(((bf16[256,224]{0,1:T(8,128)(2,1)}), bf16[256,224]{0,1:T(8,128)(2,1)}) %all-reduce.4.cloned.1.call-update) | async-done | bytes 114704 | tf_op jit(solution)/shard_map/psum | solution.py:158
  211.0 0.9 add_convert_fusion
  212.1 4.1 %gather_fusion.7 = bf16[1280,224]{1,0:T(8,128)(2,1)S(1)} fusion(bf16[128,224]{1,0:T(8,128)(2,1)S(1)} %copy.194, s32[2048]{0:T(1024)S(1)} %pad_clamp_fusion), kind=kCustom, calls=%fused_computation.7 | custom fusion | bytes 1152000 | tf_op jit(solution)/shard_map/jit(_take)/gather | solution.py:169
  216.2 1.2 select_select_fusion
  217.4 9.3 %all-to-all-start.1 = ((bf16[32,40,1,224]{3,1,2,0:T(8,128)(2,1)}), bf16[32,40,1,224]{3,1,2,0:T(8,128)(2,1)S(1)}, u32[]{:S(2)}, u32[]{:S(2)}) async-start(bf16[32,40,1,224]{3,1,2,0:T(8,128)(2,1)} %select_select_fusion), calls=%async_computation.1 | async-start | bytes 1310720 | tf_op jit(solution)/shard_map/all_to_all | solution.py:172
  226.8 17.8 %all-to-all-done.1 = bf16[32,40,1,224]{3,1,2,0:T(8,128)(2,1)S(1)} async-done(((bf16[32,40,1,224]{3,1,2,0:T(8,128)(2,1)}), bf16[32,40,1,224]{3,1,2,0:T(8,128)(2,1)S(1)}, u32[]{:S(2)}, u32[]{:S(2)}) %all-to-all-start.1) | async-done | bytes 573472 | tf_op jit(solution)/shard_map/all_to_all | solution.py:172
  244.7 0.8 copy-done.1
  245.4 1.5 copy.196
  246.9 2.1 reshape.672
  249.0 1.4 fusion.12
  250.4 2.9 fusion.91
  253.3 6.1 %convolution_convert_fusion = bf16[40,7168]{1,0:T(8,128)(2,1)} fusion(bf16[256,7168]{1,0:T(8,128)(2,1)} %param.29, bf16[7168,256]{1,0:T(8,128)(2,1)} %param.28, f32[40,256]{1,0:T(8,128)S(1)} %fusion.91, f32[40,7168]{1,0:T(8,128)S(1)} %reshape.672, f32[7168]{0:T(1024)S(1)} %copy-done.8, f32[40]{0:T(128)S(1)} %add_rsqrt_fusion), kind=kOutput, calls=%fused_computation.11 | convolution fusion | flops 294809600 | bytes 9130144 | tf_op jit(solution)/shard_map/dot_general | solution.py:182
  259.4 3.7 %convert_element_type.126 = bf16[1,40,128,56]{3,2,1,0:T(8,128)(2,1)S(1)} reshape(bf16[40,7168]{1,0:T(8,128)(2,1)} %convolution_convert_fusion) | data formatting | bytes 1146880 | tf_op jit(solution)/shard_map/convert_element_type | solution.py:184
  263.1 1.9 copy.237
  265.0 3.7 %reshape.761 = bf16[128,2,1120]{2,1,0:T(2,128)(2,1)} reshape(bf16[128,1,40,56]{3,2,1,0:T(8,128)(2,1)} %bitcast.155) | data formatting | bytes 1146880
  268.8 11.8 %all-to-all-start.2 = ((bf16[128,2,1120]{2,1,0:T(2,128)(2,1)}), bf16[128,2,1120]{2,1,0:T(2,128)(2,1)}, u32[]{:S(2)}, u32[]{:S(2)}) async-start(bf16[128,2,1120]{2,1,0:T(2,128)(2,1)} %reshape.761), calls=%async_computation.2 | async-start | bytes 1179648 | tf_op jit(solution)/shard_map/all_to_all | solution.py:183
  282.1 33.0 %gather_fusion.4 = f32[5120]{0:T(1024)S(1)} fusion(f32[128,16]{0,1:T(8,128)S(1)} %select_reduce_fusion.2, s32[5120]{0:T(1024)S(1)} %reshape.708), kind=kCustom, calls=%fused_computation.4 | custom fusion | bytes 81920 | tf_op jit(solution)/shard_map/gather | solution.py:205
  315.5 0.7 broadcast_select_fusion.1
  317.1 3.4 reshape.762
  320.5 1.7 bitcast_convert_fusion
  322.1 2.1 copy.217
  324.3 1.1 broadcast_multiply_fusion
  325.4 3.0 copy.200
  328.4 28.2 %scatter_fusion = f32[128,56]{1,0:T(8,128)S(1)} fusion(f32[128,56]{1,0:T(8,128)S(1)} %copy.199, s32[5120]{0:T(1024)S(1)} %copy-done.9, f32[5120,56]{1,0:T(8,128)} %copy.200), kind=kCustom, calls=%fused_computation.8 | custom fusion | flops 286720 | bytes 3461120 | tf_op jit(solution)/shard_map/scatter-add | solution.py:209
  (125 shorter events, 13.8 us)
Async XLA Ops:
  6.5 65.4 %copy-start = (bf16[16,512,128]{2,1,0:T(8,128)(2,1)S(1)}, bf16[16,512,128]{2,1,0:T(8,128)(2,1)}, u32[]{:S(2)}) copy-start(bf16[16,512,128]{2,1,0:T(8,128)(2,1)} %param.21) | copy-start | bytes 6291460
  11.4 13.0 %copy-start.14 = (s32[1,4]{1,0:T(1,128)S(1)}, s32[1,4]{1,0:T(1,128)}, u32[]{:S(2)}) copy-start(s32[1,4]{1,0:T(1,128)} %param.18) | copy-start | bytes 52
  11.4 13.3 %copy-start.10 = (bf16[8,576]{1,0:T(8,128)(2,1)S(1)}, bf16[8,576]{1,0:T(8,128)(2,1)}, u32[]{:S(2)}) copy-start(bf16[8,576]{1,0:T(8,128)(2,1)} %param.16) | copy-start | bytes 27652
  11.4 13.4 %copy-start.6 = (bf16[8,9216]{1,0:T(8,128)(2,1)S(1)}, bf16[8,9216]{1,0:T(8,128)(2,1)}, u32[]{:S(2)}) copy-start(bf16[8,9216]{1,0:T(8,128)(2,1)} %param.15) | copy-start | bytes 442372
  11.4 13.8 %copy-start.5 = (bf16[512,576]{0,1:T(8,128)(2,1)S(1)}, bf16[512,576]{0,1:T(8,128)(2,1)}, u32[]{:S(2)}) copy-start(bf16[512,576]{0,1:T(8,128)(2,1)} %param.17) | copy-start | bytes 1769476
  11.4 44.1 %all-to-all-start = ((bf16[32,2,16,576]{3,2,1,0:T(8,128)(2,1)}), bf16[32,2,16,576]{3,2,1,0:T(8,128)(2,1)}, u32[]{:S(2)}, u32[]{:S(2)}) async-start(bf16[32,2,16,576]{3,2,1,0:T(8,128)(2,1)} %copy.175), calls=%async_computation | async-start | bytes 2621440 | tf_op jit(solution)/shard_map/all_to_all | solution.py:97
  23.7 120.5 %all-gather.2.cloned.1.call-start = ((), (), s32[]{:S(2)}) async-start(), calls=%async_computation.3 | async-start | bytes 1081344 | tf_op jit(solution)/shard_map/all_gather | solution.py:156
  67.4 4.1 %copy-start.2 = (bf16[4,384,576]{2,1,0:T(8,128)(2,1)S(1)}, bf16[4,384,576]{2,1,0:T(8,128)(2,1)}, u32[]{:S(2)}) copy-start(bf16[4,384,576]{2,1,0:T(8,128)(2,1)} %get-tuple-element.12) | copy-start | bytes 5308420
  67.4 4.1 %copy-start.4 = (f32[4,2,16,384]{3,2,1,0:T(8,128)S(1)}, f32[4,2,16,384]{3,2,1,0:T(8,128)}, u32[]{:S(2)}) copy-start(f32[4,2,16,384]{3,2,1,0:T(8,128)} %get-tuple-element.28) | copy-start | bytes 589828
  72.0 1.4 copy-start.13
  72.0 72.2 %copy-start.3 = (bf16[2048,224]{0,1:T(8,128)(2,1)S(1)}, bf16[2048,224]{0,1:T(8,128)(2,1)}, u32[]{:S(2)}) copy-start(bf16[2048,224]{0,1:T(8,128)(2,1)} %param.22) | copy-start | bytes 2752516
  72.4 138.6 %copy-start.7 = (bf16[256,224]{0,1:T(8,128)(2,1)S(1)}, bf16[256,224]{0,1:T(8,128)(2,1)}, u32[]{:S(2)}) copy-start(bf16[256,224]{0,1:T(8,128)(2,1)} %param.23) | copy-start | bytes 344068
  73.1 137.9 %all-reduce.4.cloned.1.call-start = ((), (), s32[]{:S(2)}) async-start(), calls=%async_computation.4 | async-start | bytes 229376 | tf_op jit(solution)/shard_map/psum | solution.py:158
  217.4 27.2 %all-to-all-start.1 = ((bf16[32,40,1,224]{3,1,2,0:T(8,128)(2,1)}), bf16[32,40,1,224]{3,1,2,0:T(8,128)(2,1)S(1)}, u32[]{:S(2)}, u32[]{:S(2)}) async-start(bf16[32,40,1,224]{3,1,2,0:T(8,128)(2,1)} %select_select_fusion), calls=%async_computation.1 | async-start | bytes 1310720 | tf_op jit(solution)/shard_map/all_to_all | solution.py:172
  226.8 88.5 %copy-start.11 = (pred[128]{0:T(512)(128)(4,1)}, pred[128]{0:T(512)(128)(4,1)S(1)}, u32[]{:S(2)}) copy-start(pred[128]{0:T(512)(128)(4,1)S(1)} %compare_and_fusion.2) | copy-start | bytes 388
  244.6 0.9 copy-start.1
  246.9 3.5 copy-start.8
  265.0 16.8 %copy-start.12 = (f32[256,4]{0,1:T(4,128)S(1)}, f32[256,4]{0,1:T(4,128)}, u32[]{:S(2)}) copy-start(f32[256,4]{0,1:T(4,128)} %param.26) | copy-start | bytes 12292
  268.8 48.3 %all-to-all-start.2 = ((bf16[128,2,1120]{2,1,0:T(2,128)(2,1)}), bf16[128,2,1120]{2,1,0:T(2,128)(2,1)}, u32[]{:S(2)}, u32[]{:S(2)}) async-start(bf16[128,2,1120]{2,1,0:T(2,128)(2,1)} %reshape.761), calls=%async_computation.2 | async-start | bytes 1179648 | tf_op jit(solution)/shard_map/all_to_all | solution.py:183
  325.4 3.0 copy-start.9
Sparse Core Ops, SparseCore 0:
  73.2 70.9 all-gather.1
  146.7 64.2 all-reduce.3
where the time goes:
time: 365 us; the launch traced here: 364 us
  waiting for transfers between devices  164 us (45%)
  local copies, waits for them, and re-layouts  82.7 us (23%)
  other arithmetic  40.5 us (11%)
  starting transfers between devices  33.9 us (9%)
  matrix products  29.1 us (8%)
  between operations  14 us (4%)
    all_gather x1, waiting for transfers between devices, per_device(): lax.all_gather(values, 'attn', axis=0, tiled=True)  67.3 us
    psum x1, waiting for transfers between devices, per_device(): lax.psum(partial_cols.astype(jnp.bfloat16), ('expert', 'rep'))  64.4 us
    gather x2, local copies, waits for them, and re-layouts, per_device(): share_table[back_rows, source_expert[:, None]]  33.1 us
    scatter-add x1, other arithmetic, per_device(): jax.ops.segment_sum(weighted, back_rows.reshape(-1), num_segments=rows_part)  28.2 us
    all_to_all x1, waiting for transfers between devices, per_device(): lax.all_to_all(outgoing_rows, 'attn', split_axis=0, concat_axis=2, tiled=...  17.8 us
    all_to_all x1, waiting for transfers between devices, per_device(): lax.all_to_all(outgoing, 'attn', split_axis=0, concat_axis=0, tiled=True)  14.2 us
    all_to_all x1, starting transfers between devices, per_device(): lax.all_to_all(outgoing, 'attn', split_axis=0, concat_axis=0, tiled=True)  12.3 us
    all_to_all x1, starting transfers between devices, per_device(): lax.all_to_all(result.reshape(1, item_count, n_attn * n_expert, -1).astyp...  11.8 us
  transfers between devices with their start and end apart: 5, of which 4 were waited for; matrix products, arithmetic and copies ran while one was open for 16% of the time, Pallas kernels for 0%

commit v1 on v0

--- a/solution.py
+++ b/solution.py
@@ -155,7 +155,9 @@
     partial_cols = jnp.dot(
         lax.all_gather(values, "attn", axis=0, tiled=True), w_o, preferred_element_type=jnp.float32
     )
-    attn_cols = lax.psum(partial_cols.astype(jnp.bfloat16), ("expert", "rep")).astype(jnp.float32)
+    attn_cols = jnp.sum(
+        lax.all_gather(partial_cols.astype(jnp.bfloat16), ("expert", "rep")), axis=0
+    ).astype(jnp.float32)
     hidden_cols = (residual.astype(jnp.float32) + attn_cols).astype(jnp.bfloat16)
     rows_part = route_ids.shape[0] // n_rep
     capacity = rows_part * TOP // EXPERTS * 5 // 4

time: 365 us -> 315 us (0.86)
  waiting for transfers between devices: 164 us -> 101 us
  blocking collectives: 0 us -> 19.2 us
  starting transfers between devices: 33.9 us -> 28.1 us
    psum x1 -> x0, waiting for transfers between devices: 64.4 us -> none  [per_device(): lax.psum(partial_cols.astype(jnp.bfloat16), ('expert', 'rep'))]
    all_gather x0 -> x1, blocking collectives: none -> 19.2 us  [per_device(): lax.all_gather(partial_cols.astype(jnp.bfloat16), ('expert', 'rep'))]
    unnamed x34 -> x35, local copies, waits for them, and re-layouts: 9.59 us -> 9.82 us
  transfers between devices with their start and end apart: 5 -> 4, of which waited for: 4 -> 3; matrix products, arithmetic and copies ran while one was open for 16% -> 18% of each run, Pallas kernels for 0% -> 0%
where the time goes in v1:
time: 315 us; the launch traced here: 314 us
  waiting for transfers between devices  101 us (32%)
  local copies, waits for them, and re-layouts  82.9 us (26%)
  other arithmetic  40.3 us (13%)
  matrix products  28.5 us (9%)
  starting transfers between devices  28.1 us (9%)
  blocking collectives  19.2 us (6%)
  between operations  14.1 us (4%)
    all_gather x1, waiting for transfers between devices, per_device(): lax.all_gather(values, 'attn', axis=0, tiled=True)  67.5 us
    gather x2, local copies, waits for them, and re-layouts, per_device(): share_table[back_rows, source_expert[:, None]]  33.1 us
    scatter-add x1, other arithmetic, per_device(): jax.ops.segment_sum(weighted, back_rows.reshape(-1), num_segments=rows_part)  28.2 us
    all_gather x1, blocking collectives, per_device(): lax.all_gather(partial_cols.astype(jnp.bfloat16), ('expert', 'rep'))  19.2 us
    all_to_all x1, waiting for transfers between devices, per_device(): lax.all_to_all(outgoing_rows, 'attn', split_axis=0, concat_axis=2, tiled=...  18.9 us
    all_to_all x1, waiting for transfers between devices, per_device(): lax.all_to_all(outgoing, 'attn', split_axis=0, concat_axis=0, tiled=True)  14.2 us
    all_to_all x1, starting transfers between devices, per_device(): lax.all_to_all(outgoing, 'attn', split_axis=0, concat_axis=0, tiled=True)  12.3 us
    all_to_all x1, starting transfers between devices, per_device(): lax.all_to_all(result.reshape(1, item_count, n_attn * n_expert, -1).astyp...  9.88 us
  transfers between devices with their start and end apart: 4, of which 3 were waited for; matrix products, arithmetic and copies ran while one was open for 18% of the time, Pallas kernels for 0%

profile of v1, /device:TPU:1, one launch (start us, length us, event | category | flops | bytes accessed | tf_op | source)
XLA Modules:
  0.0 314.1 jit_solution(12295399029767563054)
XLA Ops:
  6.5 0.9 reshape.649
  7.5 0.8 convert_reduce_fusion
  8.3 1.6 convolution_convert_fusion.1
  9.9 1.5 copy.194
  11.4 12.3 %all-to-all-start = ((bf16[32,2,16,576]{3,2,1,0:T(8,128)(2,1)}), bf16[32,2,16,576]{3,2,1,0:T(8,128)(2,1)}, u32[]{:S(2)}, u32[]{:S(2)}) async-start(bf16[32,2,16,576]{3,2,1,0:T(8,128)(2,1)} %copy.194), calls=%async_computation | async-start | bytes 2621440 | tf_op jit(solution)/shard_map/all_to_all | solution.py:97
  25.0 1.1 copy.188
  26.1 2.4 gather_fusion
  28.4 1.2 concatenate.9
  30.1 8.3 %while.1 = (s32[]{:T(128)}, bf16[896,576]{1,0:T(8,128)(2,1)S(1)}, s32[4,2]{0,1:T(2,128)S(1)}, bf16[4,384,576]{2,1,0:T(8,128)(2,1)}, s32[]{:T(128)}) while((s32[]{:T(128)}, bf16[896,576]{1,0:T(8,128)(2,1)S(1)}, s32[4,2]{0,1:T(2,128)S(1)}, bf16[4,384,576]{2,1,0:T(8,128)(2,1)}, s32[]{:T(128)}) %tuple.22), condition=%wide.while_cond, body=%wide.while_body.sunk | while | flops 2 | bytes 935001 | solution.py:63
  30.9 1.5 bitcast_dynamic-update-slice_fusion.2
  32.9 1.5 bitcast_dynamic-update-slice_fusion.2
  34.9 1.4 bitcast_dynamic-update-slice_fusion.2
  36.9 1.5 bitcast_dynamic-update-slice_fusion.2
  38.4 3.0 fusion.93
  41.3 14.2 %all-to-all-done = bf16[32,2,16,576]{3,2,1,0:T(8,128)(2,1)} async-done(((bf16[32,2,16,576]{3,2,1,0:T(8,128)(2,1)}), bf16[32,2,16,576]{3,2,1,0:T(8,128)(2,1)}, u32[]{:S(2)}, u32[]{:S(2)}) %all-to-all-start) | async-done | bytes 1179680 | tf_op jit(solution)/shard_map/all_to_all | solution.py:97
  55.6 6.0 %fusion.2 = f32[64,2,16,16]{2,3,1,0:T(8,128)S(1)} fusion(bf16[64,16,576,1]{2,1,3,0:T(8,128)(2,1)} %bitcast.13, bf16[64,2,16,576]{3,2,1,0:T(8,128)(2,1)} %gather_fusion, pred[64]{0:T(512)(128)(4,1)S(1)} %compare_and_fusion.3), kind=kOutput, calls=%fused_computation.14 | convolution fusion | flops 38928384 | bytes 3670080 | tf_op jit(solution)/shard_map/nthc,nbc->nthb/dot_general | solution.py:108
  63.1 1.1 fusion.51
  64.7 0.9 copy.199
  65.5 1.9 fusion.43
  67.5 3.8 %fusion = f32[4,2,16,512]{3,0,2,1:T(4,128)S(1)} fusion(f32[64,2,16,512]{3,2,1,0:T(8,128)S(1)} %fusion.43, pred[4,64]{1,0:T(4,128)(4,1)S(1)} %fusion.81), kind=kOutput, calls=%fused_computation.12 | convolution fusion | flops 50331648 | bytes 4456704 | tf_op jit(solution)/shard_map/rn,nthc->rthc/dot_general | solution.py:147
  73.5 0.8 select_reduce_fusion
  75.1 0.8 fusion.47
  76.7 67.5 %all-gather.3.cloned.1.call-done = bf16[256,2048]{1,0:T(8,128)(2,1)} async-done(((bf16[8,2048]{1,0:T(8,128)(2,1)}), bf16[256,2048]{1,0:T(8,128)(2,1)}) %all-gather.3.cloned.1.call-update) | async-done | bytes 1048592 | tf_op jit(solution)/shard_map/all_gather | solution.py:156
  144.2 1.7 convolution_convert_fusion.2
  145.9 19.2 %all-gather = bf16[2048,224]{0,1:T(8,128)(2,1)S(1)} all-gather(bf16[256,224]{0,1:T(8,128)(2,1)S(1)} %convolution_convert_fusion.2), channel_id=2, replica_groups=mesh['attn'=32,'expert'=4,'rep'=2] {'expert','rep'}, dimensions={0}, use_global_device_ids=true | all-gather | bytes 1032192 | tf_op jit(solution)/shard_map/all_gather | solution.py:159
  166.2 4.1 %gather_fusion.7 = bf16[1280,224]{1,0:T(8,128)(2,1)S(1)} fusion(bf16[128,224]{1,0:T(8,128)(2,1)S(1)} %copy.213, s32[2048]{0:T(1024)S(1)} %pad_clamp_fusion), kind=kCustom, calls=%fused_computation.7 | custom fusion | bytes 1152000 | tf_op jit(solution)/shard_map/jit(_take)/gather | solution.py:171
  170.3 1.2 select_select_fusion
  171.5 5.9 %all-to-all-start.1 = ((bf16[32,40,1,224]{3,1,2,0:T(8,128)(2,1)}), bf16[32,40,1,224]{3,1,2,0:T(8,128)(2,1)S(1)}, u32[]{:S(2)}, u32[]{:S(2)}) async-start(bf16[32,40,1,224]{3,1,2,0:T(8,128)(2,1)} %select_select_fusion), calls=%async_computation.1 | async-start | bytes 1310720 | tf_op jit(solution)/shard_map/all_to_all | solution.py:174
  177.5 18.9 %all-to-all-done.1 = bf16[32,40,1,224]{3,1,2,0:T(8,128)(2,1)S(1)} async-done(((bf16[32,40,1,224]{3,1,2,0:T(8,128)(2,1)}), bf16[32,40,1,224]{3,1,2,0:T(8,128)(2,1)S(1)}, u32[]{:S(2)}, u32[]{:S(2)}) %all-to-all-start.1) | async-done | bytes 573472 | tf_op jit(solution)/shard_map/all_to_all | solution.py:174
  196.5 0.8 copy-done.1
  197.3 1.5 copy.215
  198.8 2.1 reshape.672
  200.9 1.4 fusion.12
  202.2 2.9 fusion.91
  205.1 6.1 %convolution_convert_fusion = bf16[40,7168]{1,0:T(8,128)(2,1)} fusion(bf16[256,7168]{1,0:T(8,128)(2,1)} %param.29, bf16[7168,256]{1,0:T(8,128)(2,1)} %param.28, f32[40,256]{1,0:T(8,128)S(1)} %fusion.91, f32[40,7168]{1,0:T(8,128)S(1)} %reshape.672, f32[7168]{0:T(1024)S(1)} %copy-done.8, f32[40]{0:T(128)S(1)} %add_rsqrt_fusion), kind=kOutput, calls=%fused_computation.11 | convolution fusion | flops 294809600 | bytes 9130144 | tf_op jit(solution)/shard_map/dot_general | solution.py:184
  211.2 3.7 %convert_element_type.128 = bf16[1,40,128,56]{3,2,1,0:T(8,128)(2,1)S(1)} reshape(bf16[40,7168]{1,0:T(8,128)(2,1)} %convolution_convert_fusion) | data formatting | bytes 1146880 | tf_op jit(solution)/shard_map/convert_element_type | solution.py:186
  215.0 1.9 copy.257
  216.9 3.7 %reshape.762 = bf16[128,2,1120]{2,1,0:T(2,128)(2,1)} reshape(bf16[128,1,40,56]{3,2,1,0:T(8,128)(2,1)} %bitcast.160) | data formatting | bytes 1146880
  220.6 9.9 %all-to-all-start.2 = ((bf16[128,2,1120]{2,1,0:T(2,128)(2,1)}), bf16[128,2,1120]{2,1,0:T(2,128)(2,1)}, u32[]{:S(2)}, u32[]{:S(2)}) async-start(bf16[128,2,1120]{2,1,0:T(2,128)(2,1)} %reshape.762), calls=%async_computation.2 | async-start | bytes 1179648 | tf_op jit(solution)/shard_map/all_to_all | solution.py:185
  232.1 33.0 %gather_fusion.4 = f32[5120]{0:T(1024)S(1)} fusion(f32[128,16]{0,1:T(8,128)S(1)} %select_reduce_fusion.2, s32[5120]{0:T(1024)S(1)} %reshape.708), kind=kCustom, calls=%fused_computation.4 | custom fusion | bytes 81920 | tf_op jit(solution)/shard_map/gather | solution.py:207
  265.4 0.7 broadcast_select_fusion.1
  266.2 0.7 reshape.740
  267.1 3.4 %reshape.763 = bf16[128,1,40,56]{3,2,1,0:T(8,128)(2,1)S(1)} reshape(bf16[128,2,1120]{2,1,0:T(2,128)(2,1)} %all-to-all-done.2) | data formatting | bytes 1146880
  270.4 1.7 bitcast_convert_fusion
  272.1 2.1 copy.236
  274.2 1.1 broadcast_multiply_fusion
  275.4 3.0 copy.219
  278.3 28.2 %scatter_fusion = f32[128,56]{1,0:T(8,128)S(1)} fusion(f32[128,56]{1,0:T(8,128)S(1)} %copy.218, s32[5120]{0:T(1024)S(1)} %copy-done.9, f32[5120,56]{1,0:T(8,128)} %copy.219), kind=kCustom, calls=%fused_computation.8 | custom fusion | flops 286720 | bytes 3461120 | tf_op jit(solution)/shard_map/scatter-add | solution.py:211
  (125 shorter events, 13.6 us)
Async XLA Ops:
  6.5 65.4 %copy-start = (bf16[16,512,128]{2,1,0:T(8,128)(2,1)S(1)}, bf16[16,512,128]{2,1,0:T(8,128)(2,1)}, u32[]{:S(2)}) copy-start(bf16[16,512,128]{2,1,0:T(8,128)(2,1)} %param.21) | copy-start | bytes 6291460
  11.4 12.8 %copy-start.14 = (s32[1,4]{1,0:T(1,128)S(1)}, s32[1,4]{1,0:T(1,128)}, u32[]{:S(2)}) copy-start(s32[1,4]{1,0:T(1,128)} %param.18) | copy-start | bytes 52
  11.4 13.1 %copy-start.10 = (bf16[8,576]{1,0:T(8,128)(2,1)S(1)}, bf16[8,576]{1,0:T(8,128)(2,1)}, u32[]{:S(2)}) copy-start(bf16[8,576]{1,0:T(8,128)(2,1)} %param.16) | copy-start | bytes 27652
  11.4 13.2 %copy-start.6 = (bf16[8,9216]{1,0:T(8,128)(2,1)S(1)}, bf16[8,9216]{1,0:T(8,128)(2,1)}, u32[]{:S(2)}) copy-start(bf16[8,9216]{1,0:T(8,128)(2,1)} %param.15) | copy-start | bytes 442372
  11.4 13.6 %copy-start.5 = (bf16[512,576]{0,1:T(8,128)(2,1)S(1)}, bf16[512,576]{0,1:T(8,128)(2,1)}, u32[]{:S(2)}) copy-start(bf16[512,576]{0,1:T(8,128)(2,1)} %param.17) | copy-start | bytes 1769476
  11.4 44.1 %all-to-all-start = ((bf16[32,2,16,576]{3,2,1,0:T(8,128)(2,1)}), bf16[32,2,16,576]{3,2,1,0:T(8,128)(2,1)}, u32[]{:S(2)}, u32[]{:S(2)}) async-start(bf16[32,2,16,576]{3,2,1,0:T(8,128)(2,1)} %copy.194), calls=%async_computation | async-start | bytes 2621440 | tf_op jit(solution)/shard_map/all_to_all | solution.py:97
  23.7 120.5 %all-gather.3.cloned.1.call-start = ((), (), s32[]{:S(2)}) async-start(), calls=%async_computation.3 | async-start | bytes 1081344 | tf_op jit(solution)/shard_map/all_gather | solution.py:156
  67.4 4.1 %copy-start.2 = (bf16[4,384,576]{2,1,0:T(8,128)(2,1)S(1)}, bf16[4,384,576]{2,1,0:T(8,128)(2,1)}, u32[]{:S(2)}) copy-start(bf16[4,384,576]{2,1,0:T(8,128)(2,1)} %get-tuple-element.12) | copy-start | bytes 5308420
  67.4 4.1 %copy-start.4 = (f32[4,2,16,384]{3,2,1,0:T(8,128)S(1)}, f32[4,2,16,384]{3,2,1,0:T(8,128)}, u32[]{:S(2)}) copy-start(f32[4,2,16,384]{3,2,1,0:T(8,128)} %get-tuple-element.28) | copy-start | bytes 589828
  72.0 1.1 copy-start.13
  72.0 72.2 %copy-start.3 = (bf16[2048,224]{0,1:T(8,128)(2,1)S(1)}, bf16[2048,224]{0,1:T(8,128)(2,1)}, u32[]{:S(2)}) copy-start(bf16[2048,224]{0,1:T(8,128)(2,1)} %param.22) | copy-start | bytes 2752516
  145.9 20.1 %copy-start.7 = (bf16[256,224]{0,1:T(8,128)(2,1)S(1)}, bf16[256,224]{0,1:T(8,128)(2,1)}, u32[]{:S(2)}) copy-start(bf16[256,224]{0,1:T(8,128)(2,1)} %param.23) | copy-start | bytes 344068
  171.5 24.9 %all-to-all-start.1 = ((bf16[32,40,1,224]{3,1,2,0:T(8,128)(2,1)}), bf16[32,40,1,224]{3,1,2,0:T(8,128)(2,1)S(1)}, u32[]{:S(2)}, u32[]{:S(2)}) async-start(bf16[32,40,1,224]{3,1,2,0:T(8,128)(2,1)} %select_select_fusion), calls=%async_computation.1 | async-start | bytes 1310720 | tf_op jit(solution)/shard_map/all_to_all | solution.py:174
  177.5 87.8 %copy-start.11 = (pred[128]{0:T(512)(128)(4,1)}, pred[128]{0:T(512)(128)(4,1)S(1)}, u32[]{:S(2)}) copy-start(pred[128]{0:T(512)(128)(4,1)S(1)} %compare_and_fusion.2) | copy-start | bytes 388
  196.4 0.9 copy-start.1
  198.7 3.5 %copy-start.8 = (f32[7168]{0:T(1024)S(1)}, f32[7168]{0:T(1024)}, u32[]{:S(2)}) copy-start(f32[7168]{0:T(1024)} %param.24) | copy-start | bytes 86020
  216.9 15.0 %copy-start.12 = (f32[256,4]{0,1:T(4,128)S(1)}, f32[256,4]{0,1:T(4,128)}, u32[]{:S(2)}) copy-start(f32[256,4]{0,1:T(4,128)} %param.26) | copy-start | bytes 12292
  220.6 46.5 %all-to-all-start.2 = ((bf16[128,2,1120]{2,1,0:T(2,128)(2,1)}), bf16[128,2,1120]{2,1,0:T(2,128)(2,1)}, u32[]{:S(2)}, u32[]{:S(2)}) async-start(bf16[128,2,1120]{2,1,0:T(2,128)(2,1)} %reshape.762), calls=%async_computation.2 | async-start | bytes 1179648 | tf_op jit(solution)/shard_map/all_to_all | solution.py:185
  275.3 3.0 copy-start.9
Sparse Core Ops, SparseCore 0:
  73.2 70.9 all-gather.2
